TPU v7x, 128 devices: a whole 4x4x4 slice. The times are simulated.
128 devices in a mesh: req: 32 (over x, z, core), tensor: 4 (over y).
Axes of the slice: x: 4, y: 4, z: 4, core: 2. Of those that a mesh axis runs over, the one named last changes fastest.
Arguments:
- hidden_in: bfloat16 [32768, 2048], P('req', 'tensor'), may hold values from -6 to 6
- segment: int32 [32768], P('req'), may hold values from 0 to 15, never falling along the last dimension, each value on 1 to 4096 neighbouring positions
- w_query: bfloat16 [2048, 1024], P(None, 'tensor'), may hold values from -0.125 to 0.125
- w_key: bfloat16 [2048, 1024], P(None, 'tensor'), may hold values from -0.125 to 0.125
- w_value: bfloat16 [2048, 2048], P(None, 'tensor'), may hold values from -0.125 to 0.125
- w_outgate: bfloat16 [2048, 2048], P(None, 'tensor'), may hold values from -0.125 to 0.125
- w_gate_down: bfloat16 [2048, 16], replicated, may hold values from -0.125 to 0.125
- w_gate_up: bfloat16 [16, 1024], P(None, 'tensor'), may hold values from -1.5 to 1.5
- gate_bias: float32 [1024], P('tensor'), may hold values from -2 to 8
- norm_gain: float32 [512], replicated, may hold values from 0.5 to 1.5
- w_out: bfloat16 [2048, 2048], P('tensor'), may hold values from -0.125 to 0.125
Outputs:
- mixed: bfloat16 [32768, 2048], P('req', 'tensor')
Inputs may be any that keep to these rules, and one draw needn't show every extreme that they name: segment never falls along the tokens; each prompt covers 1 to 4096 consecutive tokens and one covers exactly 4096.
All inputs are finite; a program needn't handle non-finite values.
Results may differ from a plain program's by a relative error of at most 0.014.
Values may be sent and summed in bfloat16 or wider, within the bound.
No kernel may reach another device: no remote copies, remote signals or barrier semaphores. Data moves between devices by JAX's collectives and lax.ppermute only.
A program may use at most 128 MiB of HBM per device.

v0:
```python
import jax
import jax.numpy as jnp
from jax import lax
from jax.sharding import PartitionSpec as P

GROUP = 64


def carried_in(shard, axis, combine, identity):
    devices, index = (lax.axis_size(axis), lax.axis_index(axis))
    everything = jax.tree.map(
        lambda part, kind: lax.all_gather(part.astype(kind), axis),
        shard,
        jax.tree.map(lambda a: jnp.bfloat16 if a.dtype == jnp.float32 else a.dtype, shard),
    )
    start = jax.tree.map(
        lambda part, zero: jnp.broadcast_to(jnp.asarray(zero, part.dtype), part.shape),
        shard,
        identity,
    )

    def lap(k, before):
        reached = k < index
        new = combine(
            before, jax.tree.map(lambda part, own: part[k].astype(own.dtype), everything, shard)
        )
        return jax.tree.map(lambda a, b: jnp.where(reached, a, b), new, before)

    return lax.fori_loop(0, devices, lap, start)


def combine(earlier, later):
    first_a, last_a, decay_a, state_a = earlier
    first_b, last_b, decay_b, state_b = later
    linked = ((first_b == last_a) | (last_a == 0.0) | (first_b == 0.0)).astype(jnp.float32)
    decay_new = decay_b * decay_a * linked
    state_new = state_b + (linked * decay_b)[:, None] * state_a
    first_new = jnp.where(first_a > 0.0, first_a, first_b)
    last_new = jnp.where(last_b > 0.0, last_b, last_a)
    return (first_new, last_new, decay_new, state_new)


def body(
    hidden_in,
    segment,
    w_query,
    w_key,
    w_value,
    w_outgate,
    w_gate_down,
    w_gate_up,
    gate_bias,
    norm_gain,
    w_out,
):
    tok_rows = hidden_in.shape[0]
    key_width = w_query.shape[1]
    value_width = w_value.shape[1]
    weights = (w_query, w_key, w_value, w_outgate, w_gate_down)
    piece = lax.all_gather(hidden_in, "tensor", axis=1, tiled=True)
    query_sum, key_sum, value_sum, outgate, low = tuple(
        (jnp.dot(piece, weight, preferred_element_type=jnp.float32) for weight in weights)
    )
    query = query_sum.astype(jnp.bfloat16)
    key = key_sum.astype(jnp.bfloat16)
    value = value_sum.astype(jnp.bfloat16)
    pre_gate = (
        jnp.dot(low, w_gate_up.astype(jnp.float32), precision=lax.Precision.HIGHEST) + gate_bias
    )
    logdecay = jax.nn.log_sigmoid(pre_gate) / 16.0
    blocks = tok_rows // GROUP
    starts = jnp.concatenate(
        [jnp.zeros((1,), jnp.int32), (segment[1:] != segment[:-1]).astype(jnp.int32)]
    )
    live_device = (jnp.cumsum(starts) == 0).astype(jnp.float32)
    seg_blocks = segment.reshape(blocks, GROUP)
    live_blocks = (jnp.cumsum(starts.reshape(blocks, GROUP), axis=1) == 0).astype(jnp.float32)
    cumul = jnp.cumsum(logdecay.reshape(blocks, GROUP, key_width), axis=1)
    block_totals = cumul[:, -1, :]
    before = jnp.cumsum(block_totals, axis=0) - block_totals
    device_cumul = (cumul + before[:, None, :]).reshape(tok_rows, key_width)
    positions = jnp.arange(GROUP)
    causal = positions[None, :] <= positions[:, None]
    middle_row = GROUP // 2

    def block_step(state, inputs):
        q_block, k_block, v_block, c_block, s_block, l_block = inputs
        q_float = q_block.astype(jnp.float32)
        k_float = k_block.astype(jnp.float32)
        v_float = v_block.astype(jnp.float32)
        inter = (
            jnp.dot(q_float * jnp.exp(c_block), state, precision=lax.Precision.HIGHEST)
            * l_block[:, None]
        )
        allowed = causal & (s_block[:, None] == s_block[None, :])
        centre = c_block[middle_row]
        q_scaled = q_float * jnp.exp(c_block - centre[None, :])
        k_scaled = k_float * jnp.exp(centre[None, :] - c_block)
        raw_scores = jnp.dot(q_scaled, k_scaled.T, precision=lax.Precision.HIGHEST)
        scores = jnp.where(allowed, raw_scores, 0.0)
        intra = jnp.dot(scores, v_float, precision=lax.Precision.HIGHEST)
        last_cumul = c_block[-1]
        same_last = (s_block == s_block[-1]).astype(jnp.float32)
        k_decayed = k_float * jnp.exp(last_cumul[None, :] - c_block) * same_last[:, None]
        state = l_block[-1] * jnp.exp(last_cumul)[:, None] * state + jnp.dot(
            k_decayed.T, v_float, precision=lax.Precision.HIGHEST
        )
        return (state, inter + intra)

    zero_state = jnp.zeros((key_width, value_width), jnp.float32)
    final_state, local_out = lax.scan(
        block_step,
        zero_state,
        (
            query.reshape(blocks, GROUP, key_width),
            key.reshape(blocks, GROUP, key_width),
            value.reshape(blocks, GROUP, value_width),
            cumul,
            seg_blocks,
            live_blocks,
        ),
    )
    local_out = local_out.reshape(tok_rows, value_width)
    first_id = (segment[0] + 1).astype(jnp.float32)
    last_id = (segment[-1] + 1).astype(jnp.float32)
    decay_device = jnp.exp(device_cumul[-1]) * live_device[-1]
    mine = (first_id, last_id, decay_device, final_state)
    identity = (
        jnp.zeros((), jnp.float32),
        jnp.zeros((), jnp.float32),
        jnp.ones((key_width,), jnp.float32),
        jnp.zeros((key_width, value_width), jnp.float32),
    )
    incoming = carried_in(mine, "req", combine, identity)
    first_in, last_in, decay_in, state_in = incoming
    linked = ((first_id == last_in) | (last_in == 0.0)).astype(jnp.float32)
    carried = jnp.dot(
        query.astype(jnp.float32) * jnp.exp(device_cumul), state_in, precision=lax.Precision.HIGHEST
    )
    attn = (local_out + carried * (live_device * linked)[:, None]) * key_width ** (-0.5)
    normed = attn * lax.rsqrt(jnp.mean(attn * attn, axis=-1, keepdims=True) + 1e-05) * norm_gain
    gated = (normed * jax.nn.silu(outgate)).astype(jnp.bfloat16)
    head_term = jnp.dot(gated, w_out, preferred_element_type=jnp.float32)
    return lax.psum_scatter(
        head_term.astype(jnp.bfloat16), "tensor", scatter_dimension=1, tiled=True
    )


def solution(mesh):
    in_specs = (
        P("req", "tensor"),
        P("req"),
        P(None, "tensor"),
        P(None, "tensor"),
        P(None, "tensor"),
        P(None, "tensor"),
        P(),
        P(None, "tensor"),
        P("tensor"),
        P(),
        P("tensor", None),
    )
    out_specs = P("req", "tensor")
    return jax.shard_map(body, mesh=mesh, in_specs=in_specs, out_specs=out_specs, check_vma=False)
```

profile of v0, /device:TPU:1, one launch (start us, length us, event | category | flops | bytes accessed | tf_op | source)
XLA Modules:
  0.0 539.6 jit_solution(2485547177089798620)
XLA Ops:
  9.3 51.0 %all-gather.5.cloned.1.call-done = bf16[1024,2048]{1,0:T(8,128)(2,1)} async-done(((bf16[1024,512]{1,0:T(8,128)(2,1)}), bf16[1024,2048]{1,0:T(8,128)(2,1)}) %all-gather.5.cloned.1.call-update) | async-done | bytes 4194320 | tf_op jit(solution)/shard_map/all_gather | solution.py:60
  60.3 3.4 fusion.69
  63.7 1.2 fusion.48
  64.9 1.6 fusion.49
  66.5 1.3 convolution_convert_fusion.2
  68.0 3.4 convolution_convert_fusion.1
  71.4 2.0 convolution_convert_fusion.3
  73.5 133.2 %while.29 = (s32[]{:T(128)}, f32[256,512]{1,0:T(8,128)S(1)}, f32[16,64,512]{2,1,0:T(8,128)}, f32[16,64]{1,0:T(8,128)S(1)}, f32[16,64,256]{2,0,1:T(8,128)}, /*ind...) while((s32[]{:T(128)}, f32[256,512]{1,0:T(8,128)S(1)}, ...), condition=%wide.region_3.4_spmd.clone, body=%wide.region_2.3_spmd.clone.sunk | while | flops 239878528 | bytes 2676648 | solution.py:111
  73.5 1.1 constant_dynamic-slice_fusion.6
  76.7 1.1 fusion.114
  80.4 1.4 convolution_add_fusion.3
  81.8 1.1 constant_dynamic-slice_fusion.6
  85.0 1.1 fusion.114
  88.7 1.4 convolution_add_fusion.3
  90.1 1.1 constant_dynamic-slice_fusion.6
  93.3 1.1 fusion.114
  97.0 1.4 convolution_add_fusion.3
  98.4 1.1 constant_dynamic-slice_fusion.6
  101.6 1.1 fusion.114
  105.3 1.4 convolution_add_fusion.3
  106.8 1.1 constant_dynamic-slice_fusion.6
  110.0 1.1 fusion.114
  113.7 1.4 convolution_add_fusion.3
  115.1 1.1 constant_dynamic-slice_fusion.6
  118.3 1.1 fusion.114
  122.0 1.4 convolution_add_fusion.3
  123.4 1.1 constant_dynamic-slice_fusion.6
  126.6 1.1 fusion.114
  130.3 1.4 convolution_add_fusion.3
  131.7 1.1 constant_dynamic-slice_fusion.6
  134.9 1.1 fusion.114
  138.6 1.4 convolution_add_fusion.3
  140.1 1.1 constant_dynamic-slice_fusion.6
  143.3 1.1 fusion.114
  147.0 1.4 convolution_add_fusion.3
  148.4 1.1 constant_dynamic-slice_fusion.6
  151.6 1.1 fusion.114
  155.3 1.4 convolution_add_fusion.3
  159.9 1.1 fusion.114
  163.6 1.4 convolution_add_fusion.3
  165.1 1.1 constant_dynamic-slice_fusion.6
  168.2 1.1 fusion.114
  171.9 1.4 convolution_add_fusion.3
  173.4 1.1 constant_dynamic-slice_fusion.6
  176.6 1.1 fusion.114
  180.2 1.4 convolution_add_fusion.3
  184.9 1.1 fusion.114
  188.6 1.4 convolution_add_fusion.3
  190.0 1.1 constant_dynamic-slice_fusion.6
  193.2 1.1 fusion.114
  196.9 1.4 convolution_add_fusion.3
  198.3 1.1 constant_dynamic-slice_fusion.6
  201.5 1.1 fusion.114
  205.2 1.4 convolution_add_fusion.3
  207.5 1.4 fusion.66
  211.0 1.4 dynamic-update-slice
  212.4 63.8 %all-reduce.2 = (bf16[32]{0:T(256)(128)(2,1)S(1)}, bf16[32]{0:T(256)(128)(2,1)S(1)}) all-reduce(bf16[32]{0:T(256)(128)(2,1)S(1)} %dynamic-update-slice, bf16[32]{0:T(256)(128)(2,1)S(1)} %dynamic-update-slice.1), channel_id=1, replica_groups=mesh['req'=32,'tensor'=4] {'req'}, use_global_device_ids=true, to_apply=%add | all-reduce | flops 64 | bytes 256
  279.6 1.3 broadcast_add_fusion
  282.5 25.4 %all-gather.1 = bf16[32,1,256]{2,1,0:T(2,128)(2,1)S(1)} all-gather(bf16[1,1,256]{2,1,0:T(2,128)(2,1)S(1)} %fusion.62), channel_id=1, replica_groups=mesh['req'=32,'tensor'=4] {'req'}, dimensions={0}, use_global_device_ids=true | all-gather | bytes 16896 | tf_op jit(solution)/shard_map/all_gather | solution.py:12
  307.9 2.9 copy.41
  310.8 160.3 %while.30 = (s32[]{:T(128)}, f32[]{:T(128)}, f32[256,512]{1,0:T(8,128)S(1)}, s32[]{:T(128)}, bf16[32]{0:T(256)(128)(2,1)S(1)}, /*index=5*/bf16[32,256,512]{2,1,0...) while((s32[]{:T(128)}, f32[]{:T(128)}, ...), condition=%wide.region_8.9_spmd.clone, body=%wide.region_7.8_spmd.clone.sunk | while | flops 655885 | bytes 1313502 | solution.py:29
  471.2 5.6 %multiply_reduce_fusion = (f32[1024]{0:T(1024)S(1)}, f32[1024,512]{0,1:T(8,128)}) fusion(f32[1024,512]{0,1:T(8,128)} %copy.41, f32[1024]{0:T(1024)S(1)} %select_bitcast_fusion, f32[256,512]{1,0:T(8,128)S(1)} %get-tuple-element.200, f32[1024,256]{1,0:T(8,128)} %bitcast.116, bf16[1024,256]{1,0:T(8,128)(2,1)S(1)} %bitcast.119), kind=kOutput, calls=%fused_computation.59 | convolution fusion | flops 1613757440 | bytes 6299648 | tf_op jit(solution)/shard_map/dot_general | solution.py:137
  476.8 10.3 %convolution_convert_fusion = bf16[1024,2048]{1,0:T(8,128)(2,1)} fusion(bf16[512,2048]{1,0:T(8,128)(2,1)S(1)} %copy-done, f32[1024,512]{0,1:T(8,128)} %get-tuple-element.340, f32[512]{0:T(512)S(1)} %copy-done.7, f32[1024]{0:T(1024)S(1)} %rsqrt_multiply_fusion, bf16[1024,2048]{1,0:T(8,128)(2,1)} %all-gather.5.cloned.1.call-done, bf16[2048,512]{1,0:T(8,128)(2,1)} %param.20), kind=kOutput, calls=%fused_computation.56 | convolution fusion | flops 4301258752 | bytes 14686208 | tf_op jit(solution)/shard_map/dot_general | solution.py:143
  487.2 46.0 %reduce-scatter.2.cloned.1.call-done = bf16[1024,512]{1,0:T(8,128)(2,1)} async-done(((bf16[1024,2048]{1,0:T(8,128)(2,1)}), bf16[1024,512]{1,0:T(8,128)(2,1)}) %reduce-scatter.2.cloned.1.call-update) | async-done | bytes 1048592 | tf_op jit(solution)/shard_map/reduce_scatter | solution.py:144
  (393 shorter events, 162.6 us)
Async XLA Ops:
  6.5 470.3 %copy-start = (bf16[512,2048]{1,0:T(8,128)(2,1)S(1)}, bf16[512,2048]{1,0:T(8,128)(2,1)}, u32[]{:S(2)}) copy-start(bf16[512,2048]{1,0:T(8,128)(2,1)} %param.25) | copy-start | bytes 6291460
  6.5 53.7 %all-gather.5.cloned.1.call-start = ((), (), s32[]{:S(2)}) async-start(), calls=%async_computation.1 | async-start | bytes 5242880 | tf_op jit(solution)/shard_map/all_gather | solution.py:60
  7.3 303.5 %all-gather.7.cloned.1.call-start = ((), (), s32[]{:S(2)}) async-start(), calls=%async_computation.3 | async-start | bytes 8650752 | tf_op jit(solution)/shard_map/all_gather | solution.py:12
  9.3 54.4 %copy-start.6 = (bf16[16,256]{1,0:T(8,128)(2,1)S(1)}, bf16[16,256]{1,0:T(8,128)(2,1)}, u32[]{:S(2)}) copy-start(bf16[16,256]{1,0:T(8,128)(2,1)} %param.22) | copy-start | bytes 24580
  9.3 54.4 %copy-start.8 = (f32[256]{0:T(256)S(1)}, f32[256]{0:T(256)}, u32[]{:S(2)}) copy-start(f32[256]{0:T(256)} %param.23) | copy-start | bytes 3076
  63.7 2.8 copy-start.1
  63.7 2.8 copy-start.4
  66.4 1.6 copy-start.3
  68.0 3.4 copy-start.5
  73.5 136.1 %copy-start.9 = (u32[128]{0:T(128)S(1)}, u32[128]{0:T(128)}, u32[]{:S(2)}) copy-start(u32[128]{0:T(128)} %constant.99) | copy-start | bytes 1540
  207.4 325.7 %reduce-scatter.2.cloned.1.call-start = ((), (), s32[]{:S(2)}) async-start(), calls=%async_computation.2 | async-start | bytes 5242880 | tf_op jit(solution)/shard_map/reduce_scatter | solution.py:144
  281.5 1.0 copy-start.2
  471.2 5.6 %copy-start.7 = (f32[512]{0:T(512)S(1)}, f32[512]{0:T(512)}, u32[]{:S(2)}) copy-start(f32[512]{0:T(512)} %param.24) | copy-start | bytes 6148
Sparse Core Ops, SparseCore 0:
  9.0 51.2 all-gather.4
  207.5 53.9 all-gather.6
  487.3 45.7 reduce-scatter.1
where the time goes:
time: 546 us; the launch traced here: 540 us
  matrix products  99.8 us (18%)
  waiting for transfers between devices  97.7 us (18%)
  local copies, waits for them, and re-layouts  90.8 us (17%)
  blocking collectives  89.2 us (16%)
  loops' own time  84.8 us (16%)
  other arithmetic  62.7 us (11%)
  between operations  14.6 us (3%)
    another operation x1, loops' own time, carried_in(): return lax.fori_loop(0, devices, lap, start)  83.2 us
    unnamed x1, blocking collectives  63.8 us
    all_gather x1, waiting for transfers between devices, body(): piece = lax.all_gather(hidden_in, 'tensor', axis=1, tiled=True)  51 us
    reduce_scatter x1, waiting for transfers between devices, body(): lax.psum_scatter(head_term.astype(jnp.bfloat16), 'tensor', scatter_dimens...  46 us
    dynamic_slice x64, local copies, waits for them, and re-layouts, lap(): part[k].astype(own.dtype)  41.7 us
    select_n x32, other arithmetic, lap(): return jax.tree.map(lambda a, b: jnp.where(reached, a, b), new, before)  34.9 us
    all_gather x1, blocking collectives, carried_in(): lax.all_gather(part.astype(kind), axis)  25.4 us
    dot_general x16, matrix products, block_step(): jnp.dot(k_decayed.T, v_float, precision=lax.Precision.HIGHEST)  22.6 us
  transfers between devices with their start and end apart: 3, of which 2 were waited for; matrix products, arithmetic and copies ran while one was open for 3% of the time, Pallas kernels for 0%

commit v1 on v0

--- a/solution.py
+++ b/solution.py
@@ -57,7 +57,11 @@
     key_width = w_query.shape[1]
     value_width = w_value.shape[1]
     weights = (w_query, w_key, w_value, w_outgate, w_gate_down)
-    piece = lax.all_gather(hidden_in, "tensor", axis=1, tiled=True)
+    name_strings = lambda xs: jnp.concatenate(
+        lax.all_to_all(jnp.stack([xs for _ in range(lax.axis_size("tensor"))]), "tensor", 0, 0),
+        axis=1,
+    )
+    piece = name_strings(hidden_in)
     query_sum, key_sum, value_sum, outgate, low = tuple(
         (jnp.dot(piece, weight, preferred_element_type=jnp.float32) for weight in weights)
     )

time: 546 us -> 556 us (1.018)
  matrix products: 99.8 us -> 106 us
    all_gather x1 -> x0, waiting for transfers between devices: 51 us -> none  [body(): piece = lax.all_gather(hidden_in, 'tensor', axis=1, tiled=True)]
    all_to_all x0 -> x1, waiting for transfers between devices: none -> 48.3 us  [body(): lax.all_to_all(jnp.stack([xs for _ in range(lax.axis_size('tensor'))]), '...]
    dot_general x4, matrix products: 10 us -> 16.5 us  [body(): jnp.dot(piece, weight, preferred_element_type=jnp.float32)]
  transfers between devices with their start and end apart: 3 -> 3, of which waited for: 2 -> 2; matrix products, arithmetic and copies ran while one was open for 3% -> 2% of each run, Pallas kernels for 0% -> 0%
where the time goes in v1:
time: 556 us; the launch traced here: 550 us
  matrix products  106 us (19%)
  local copies, waits for them, and re-layouts  93.9 us (17%)
  waiting for transfers between devices  93.5 us (17%)
  blocking collectives  90.5 us (16%)
  loops' own time  84.8 us (15%)
  other arithmetic  61.2 us (11%)
  between operations  14.9 us (3%)
    another operation x1, loops' own time, carried_in(): return lax.fori_loop(0, devices, lap, start)  83.2 us
    unnamed x1, blocking collectives  65.9 us
    all_to_all x1, waiting for transfers between devices, body(): lax.all_to_all(jnp.stack([xs for _ in range(lax.axis_size('tensor'))]), '...  48.3 us
    reduce_scatter x1, waiting for transfers between devices, body(): lax.psum_scatter(head_term.astype(jnp.bfloat16), 'tensor', scatter_dimens...  45.1 us
    dynamic_slice x64, local copies, waits for them, and re-layouts, lap(): part[k].astype(own.dtype)  41.7 us
    select_n x32, other arithmetic, lap(): return jax.tree.map(lambda a, b: jnp.where(reached, a, b), new, before)  34.9 us
    all_gather x1, blocking collectives, carried_in(): lax.all_gather(part.astype(kind), axis)  24.6 us
    dot_general x16, matrix products, block_step(): jnp.dot(k_decayed.T, v_float, precision=lax.Precision.HIGHEST)  22.6 us
  transfers between devices with their start and end apart: 3, of which 2 were waited for; matrix products, arithmetic and copies ran while one was open for 2% of the time, Pallas kernels for 0%

profile of v1, /device:TPU:1, one launch (start us, length us, event | category | flops | bytes accessed | tf_op | source)
XLA Modules:
  0.0 550.1 jit_solution(12630388079054616347)
XLA Ops:
  6.5 1.6 copy.38
  8.2 2.5 stack.2
  10.7 5.1 all-to-all-start
  16.3 48.3 %all-to-all-done = bf16[4,1024,512]{1,2,0:T(8,128)(2,1)} async-done(((bf16[4,1024,512]{1,2,0:T(8,128)(2,1)}), bf16[4,1024,512]{1,2,0:T(8,128)(2,1)}, u32[]{:S(2)}, u32[]{:S(2)}) %all-to-all-start) | async-done | bytes 4194336 | tf_op jit(solution)/shard_map/all_to_all | solution.py:61
  64.7 2.9 fusion.69
  67.6 1.2 fusion.48
  68.7 1.6 fusion.49
  70.3 3.7 convolution_convert_fusion.2
  74.0 5.7 %convolution_convert_fusion.1 = bf16[1024,512]{1,0:T(8,128)(2,1)} fusion(bf16[1024,2048]{0,1:T(8,128)(2,1)} %bitcast.1, bf16[2048,512]{1,0:T(8,128)(2,1)S(1)} %copy-done.4), kind=kOutput, calls=%fused_computation.61 | convolution fusion | flops 2148007936 | bytes 7340032 | tf_op jit(solution)/shard_map/dot_general | solution.py:66
  79.7 4.3 convolution_convert_fusion.3
  84.0 133.2 %while.29 = (s32[]{:T(128)}, f32[256,512]{1,0:T(8,128)S(1)}, f32[16,64,512]{2,1,0:T(8,128)}, f32[16,64]{1,0:T(8,128)S(1)}, f32[16,64,256]{2,0,1:T(8,128)}, /*ind...) while((s32[]{:T(128)}, f32[256,512]{1,0:T(8,128)S(1)}, ...), condition=%wide.region_3.4_spmd.clone, body=%wide.region_2.3_spmd.clone.sunk | while | flops 239878528 | bytes 2676648 | solution.py:115
  84.0 1.1 constant_dynamic-slice_fusion.6
  87.2 1.1 fusion.114
  90.9 1.4 convolution_add_fusion.3
  95.5 1.1 fusion.114
  99.2 1.4 convolution_add_fusion.3
  100.6 1.1 constant_dynamic-slice_fusion.6
  103.8 1.1 fusion.114
  107.5 1.4 convolution_add_fusion.3
  109.0 1.1 constant_dynamic-slice_fusion.6
  112.2 1.1 fusion.114
  115.9 1.4 convolution_add_fusion.3
  117.3 1.1 constant_dynamic-slice_fusion.6
  120.5 1.1 fusion.114
  124.2 1.4 convolution_add_fusion.3
  125.6 1.1 constant_dynamic-slice_fusion.6
  128.8 1.1 fusion.114
  132.5 1.4 convolution_add_fusion.3
  137.1 1.1 fusion.114
  140.8 1.4 convolution_add_fusion.3
  145.5 1.1 fusion.114
  149.2 1.4 convolution_add_fusion.3
  150.6 1.1 constant_dynamic-slice_fusion.6
  153.8 1.1 fusion.114
  157.5 1.4 convolution_add_fusion.3
  162.1 1.1 fusion.114
  165.8 1.4 convolution_add_fusion.3
  167.2 1.1 constant_dynamic-slice_fusion.6
  170.4 1.1 fusion.114
  174.1 1.4 convolution_add_fusion.3
  175.6 1.1 constant_dynamic-slice_fusion.6
  178.8 1.1 fusion.114
  182.5 1.4 convolution_add_fusion.3
  183.9 1.1 constant_dynamic-slice_fusion.6
  187.1 1.1 fusion.114
  190.8 1.4 convolution_add_fusion.3
  192.2 1.1 constant_dynamic-slice_fusion.6
  195.4 1.1 fusion.114
  199.1 1.4 convolution_add_fusion.3
  200.5 1.1 constant_dynamic-slice_fusion.6
  203.7 1.1 fusion.114
  207.4 1.4 convolution_add_fusion.3
  208.8 1.1 constant_dynamic-slice_fusion.6
  212.0 1.1 fusion.114
  215.7 1.4 convolution_add_fusion.3
  220.7 1.4 dynamic-update-slice
  222.1 65.9 %all-reduce.2 = (bf16[32]{0:T(256)(128)(2,1)S(1)}, bf16[32]{0:T(256)(128)(2,1)S(1)}) all-reduce(bf16[32]{0:T(256)(128)(2,1)S(1)} %dynamic-update-slice, bf16[32]{0:T(256)(128)(2,1)S(1)} %dynamic-update-slice.1), channel_id=1, replica_groups=mesh['req'=32,'tensor'=4] {'req'}, use_global_device_ids=true, to_apply=%add | all-reduce | flops 64 | bytes 256
  291.4 1.3 broadcast_add_fusion
  294.3 24.6 %all-gather.1 = bf16[32,1,256]{2,1,0:T(2,128)(2,1)S(1)} all-gather(bf16[1,1,256]{2,1,0:T(2,128)(2,1)S(1)} %fusion.62), channel_id=1, replica_groups=mesh['req'=32,'tensor'=4] {'req'}, dimensions={0}, use_global_device_ids=true | all-gather | bytes 16896 | tf_op jit(solution)/shard_map/all_gather | solution.py:12
  318.9 2.9 copy.44
  321.8 160.3 %while.30 = (s32[]{:T(128)}, f32[]{:T(128)}, f32[256,512]{1,0:T(8,128)S(1)}, s32[]{:T(128)}, bf16[32]{0:T(256)(128)(2,1)S(1)}, /*index=5*/bf16[32,256,512]{2,1,0...) while((s32[]{:T(128)}, f32[]{:T(128)}, ...), condition=%wide.region_8.9_spmd.clone, body=%wide.region_7.8_spmd.clone.sunk | while | flops 655885 | bytes 1313502 | solution.py:29
  482.2 5.6 %multiply_reduce_fusion = (f32[1024]{0:T(1024)S(1)}, f32[1024,512]{0,1:T(8,128)}) fusion(f32[1024,512]{0,1:T(8,128)} %copy.44, f32[1024]{0:T(1024)S(1)} %select_bitcast_fusion, f32[256,512]{1,0:T(8,128)S(1)} %get-tuple-element.200, f32[1024,256]{1,0:T(8,128)} %bitcast.119, bf16[1024,256]{1,0:T(8,128)(2,1)S(1)} %bitcast.122), kind=kOutput, calls=%fused_computation.59 | convolution fusion | flops 1613757440 | bytes 6299648 | tf_op jit(solution)/shard_map/dot_general | solution.py:141
  487.8 10.3 %convolution_convert_fusion = bf16[1024,2048]{1,0:T(8,128)(2,1)} fusion(bf16[512,2048]{1,0:T(8,128)(2,1)S(1)} %copy-done, f32[1024,512]{0,1:T(8,128)} %get-tuple-element.340, f32[512]{0:T(512)S(1)} %copy-done.8, f32[1024]{0:T(1024)S(1)} %rsqrt_multiply_fusion, bf16[1024,2048]{0,1:T(8,128)(2,1)} %bitcast.1, bf16[2048,512]{1,0:T(8,128)(2,1)} %param.20), kind=kOutput, calls=%fused_computation.56 | convolution fusion | flops 4301258752 | bytes 14686208 | tf_op jit(solution)/shard_map/dot_general | solution.py:147
  498.1 45.1 %reduce-scatter.2.cloned.1.call-done = bf16[1024,512]{1,0:T(8,128)(2,1)} async-done(((bf16[1024,2048]{1,0:T(8,128)(2,1)}), bf16[1024,512]{1,0:T(8,128)(2,1)}) %reduce-scatter.2.cloned.1.call-update) | async-done | bytes 1048592 | tf_op jit(solution)/shard_map/reduce_scatter | solution.py:148
  (396 shorter events, 162.9 us)
Async XLA Ops:
  6.5 481.3 %copy-start = (bf16[512,2048]{1,0:T(8,128)(2,1)S(1)}, bf16[512,2048]{1,0:T(8,128)(2,1)}, u32[]{:S(2)}) copy-start(bf16[512,2048]{1,0:T(8,128)(2,1)} %param.25) | copy-start | bytes 6291460
  10.6 5.1 copy-start.3
  10.7 54.0 %copy-start.2 = (bf16[2048,16]{0,1:T(8,128)(2,1)S(1)}, bf16[2048,16]{0,1:T(8,128)(2,1)}, u32[]{:S(2)}) copy-start(bf16[2048,16]{0,1:T(8,128)(2,1)} %param.21) | copy-start | bytes 196612
  10.7 54.0 %all-to-all-start = ((bf16[4,1024,512]{1,2,0:T(8,128)(2,1)}), bf16[4,1024,512]{1,2,0:T(8,128)(2,1)}, u32[]{:S(2)}, u32[]{:S(2)}) async-start(bf16[4,1024,512]{1,2,0:T(8,128)(2,1)} %stack.2), calls=%async_computation | async-start | bytes 8388608 | tf_op jit(solution)/shard_map/all_to_all | solution.py:61
  15.8 306.0 %all-gather.4.cloned.1.call-start = ((), (), s32[]{:S(2)}) async-start(), calls=%async_computation.3 | async-start | bytes 8650752 | tf_op jit(solution)/shard_map/all_gather | solution.py:12
  64.7 2.9 copy-start.7
  64.7 2.9 copy-start.9
  67.5 2.8 copy-start.5
  70.3 3.7 copy-start.4
  74.0 5.7 %copy-start.6 = (bf16[2048,256]{1,0:T(8,128)(2,1)S(1)}, bf16[2048,256]{1,0:T(8,128)(2,1)}, u32[]{:S(2)}) copy-start(bf16[2048,256]{1,0:T(8,128)(2,1)} %param.18) | copy-start | bytes 3145732
  84.0 135.3 %copy-start.10 = (u32[128]{0:T(128)S(1)}, u32[128]{0:T(128)}, u32[]{:S(2)}) copy-start(u32[128]{0:T(128)} %constant.99) | copy-start | bytes 1540
  217.9 325.4 %reduce-scatter.2.cloned.1.call-start = ((), (), s32[]{:S(2)}) async-start(), calls=%async_computation.2 | async-start | bytes 5242880 | tf_op jit(solution)/shard_map/reduce_scatter | solution.py:148
  293.3 1.0 copy-start.1
  482.2 5.6 %copy-start.8 = (f32[512]{0:T(512)S(1)}, f32[512]{0:T(512)}, u32[]{:S(2)}) copy-start(f32[512]{0:T(512)} %param.24) | copy-start | bytes 6148
Sparse Core Ops, SparseCore 0:
  218.0 54.8 all-gather.3
  498.3 44.9 reduce-scatter.1
